TPU v7x, 32 devices: a whole 2x2x4 slice. The times are simulated.
32 devices in a mesh: dp: 16 (over z, x, core), vocab: 2 (over y).
Axes of the slice: x: 2, y: 2, z: 4, core: 2. Of those that a mesh axis runs over, the one named last changes fastest.
Arguments:
- hidden: bfloat16 [2048, 8192], P('dp', 'vocab')
- rank_factor: bfloat16 [256, 8192], P(None, 'vocab'), may hold values from -0.0625 to 0.0625
- vocab_factor: bfloat16 [256, 77824], P('dp', 'vocab')
- lengths: int32 [2048], P('dp'), may hold values from 0 to 4096, as said below
- targets: int32 [2048], P('dp'), may hold values from 0 to 77823
- cotangent: bfloat16 [2048], P('dp'), may hold values from -96 to 96
- grammar: int32 [64, 22], P('dp', 'vocab'), may hold values from 0 to 1073741823, as said below
- assign: int32 [2048], P('dp'), may hold values from 0 to 127, as said below
Outputs:
- grad_hidden: bfloat16 [2048, 8192], P('dp', 'vocab')
- grad_factor: float32 [256, 8192], P('dp', 'vocab')
Inputs may be any that keep to these rules, and one draw needn't show every extreme that they name: `lengths`: in each aligned block of 128 rows the rows with a length above 0 come first; in every draw one such block has all 128 rows above 0 and a row of length 4096. `grammar`: only bits 0 to 29 of a word are used. `assign`: each aligned block of 128 entries is a permutation of 0 to 127.
All inputs are finite; a program needn't handle non-finite values.
Results may differ from a plain program's by a relative error of at most 0.0085.
Values may be sent and summed in bfloat16 or wider, within the bound.
No kernel may reach another device: no remote copies, remote signals or barrier semaphores. Data moves between devices by JAX's collectives and lax.ppermute only.
A program may use at most 128 MiB of HBM per device.

v0:
```python
import jax
import jax.numpy as jnp
from jax import lax
from jax.sharding import PartitionSpec as P

PREFIX_MAX = 4096
far_below = -1e30


def body(hidden, rank_factor, vocab_factor, lengths, targets, cotangent, grammar, assign):
    row_count = hidden.shape[0]
    rank = rank_factor.shape[0]
    groups = lax.axis_size("dp")
    share = row_count // groups
    width = vocab_factor.shape[1]
    tiles = width // 128
    first = lax.axis_index("vocab") * width
    factor = lax.all_gather(vocab_factor, "dp", axis=0, tiled=True)
    row_words = jnp.repeat(grammar, row_count // grammar.shape[0], axis=0)
    weight = cotangent.astype(jnp.float32) * lengths.astype(jnp.float32) / PREFIX_MAX
    partial_latent = lax.dot_general(
        hidden, rank_factor, (((1,), (1,)), ((), ())), preferred_element_type=jnp.float32
    )
    latent = lax.psum(partial_latent, "vocab").astype(jnp.bfloat16)
    target_local = targets - first
    columns = jnp.arange(width, dtype=jnp.int32)
    shifts = jnp.arange(30, dtype=jnp.int32)
    logits = jnp.dot(latent, factor, preferred_element_type=jnp.float32)
    bits = jnp.right_shift(row_words[:, :, None], shifts) & 1
    bits = bits.reshape(row_count, -1)[:, :tiles]
    tile_on = jnp.broadcast_to((bits == 1)[:, :, None], (row_count, tiles, 128)).reshape(
        row_count, width
    )
    target_hit = columns[None, :] == target_local[:, None]
    allowed = tile_on | target_hit
    masked = jnp.where(allowed, logits, far_below)
    peak = lax.pmax(jnp.max(masked, axis=1), "vocab")
    powers = jnp.where(allowed, jnp.exp(masked - peak[:, None]), 0.0)
    total = lax.psum(jnp.sum(powers, axis=1), "vocab")
    row_probs = powers / total[:, None]
    score_grad = (weight[:, None] * (row_probs - target_hit.astype(jnp.float32))).astype(
        jnp.bfloat16
    )
    rank_partial = lax.dot_general(
        score_grad, factor, (((1,), (1,)), ((), ())), preferred_element_type=jnp.float32
    )
    rank_grad = lax.psum(rank_partial, "vocab").astype(jnp.bfloat16)
    grad_factor = lax.psum_scatter(
        lax.dot_general(
            rank_grad, hidden, (((0,), (0,)), ((), ())), preferred_element_type=jnp.float32
        ).astype(jnp.bfloat16),
        "dp",
        scatter_dimension=0,
        tiled=True,
    ).astype(jnp.float32)
    picked = jnp.take(rank_grad, assign, axis=0).reshape(groups, share, rank)
    slot_rank = lax.all_to_all(picked, "dp", split_axis=0, concat_axis=0, tiled=True).reshape(
        row_count, rank
    )
    grad_hidden = jnp.dot(slot_rank, rank_factor, preferred_element_type=jnp.float32).astype(
        jnp.bfloat16
    )
    return (grad_hidden, grad_factor)


def solution(mesh):
    return jax.shard_map(
        body,
        mesh=mesh,
        in_specs=(
            P("dp", "vocab"),
            P(None, "vocab"),
            P("dp", "vocab"),
            P("dp"),
            P("dp"),
            P("dp"),
            P("dp", "vocab"),
            P("dp"),
        ),
        out_specs=(P("dp", "vocab"), P("dp", "vocab")),
        check_vma=False,
    )
```

profile of v0, /device:TPU:0, one launch (start us, length us, event | category | flops | bytes accessed | tf_op | source)
XLA Modules:
  0.0 263.4 jit_solution(1974408419297866180)
XLA Ops:
  7.2 0.0 copy-start
  7.2 0.0 all-gather.2.cloned.1.call-start
  7.2 0.7 all-gather.2.cloned.1.call-update
  7.9 0.0 reduce-scatter.2.cloned.1.call-start
  8.0 0.8 copy.10
  8.7 0.1 broadcast_in_dim.38
  8.8 0.1 shift_right_arithmetic.22
  9.0 0.1 shift_right_arithmetic.26
  9.0 0.1 fusion.4
  9.2 0.2 copy.11
  9.3 0.0 copy-done
  9.3 2.1 fusion.10
  11.4 11.4 %all-reduce.2 = bf16[128,256]{1,0:T(8,128)(2,1)S(1)} all-reduce(f32[128,256]{1,0:T(8,128)S(1)} %fusion.10), channel_id=1, replica_groups=mesh['dp'=16,'vocab'=2] {'vocab'}, use_global_device_ids=true, to_apply=%region_0.0 | all-reduce | flops 32768 | bytes 196608 | tf_op jit(solution)/shard_map/psum | solution.py:24
  22.9 0.7 broadcast_subtract_fusion
  23.5 0.7 multiply_multiply_fusion
  24.2 92.0 %all-gather.2.cloned.1.call-done = bf16[256,38912]{1,0:T(8,128)(2,1)} async-done(((bf16[16,38912]{1,0:T(8,128)(2,1)}), bf16[256,38912]{1,0:T(8,128)(2,1)}) %all-gather.2.cloned.1.call-update) | async-done | bytes 19922960 | tf_op jit(solution)/shard_map/all_gather | solution.py:18
  116.2 6.6 %broadcast_in_dim.39 = pred[128,304,128]{2,1,0:T(8,128)(4,1)S(1)} broadcast(pred[128,304]{1,0:T(8,128)(4,1)S(1)} %copy.11), dimensions={0,1} | broadcast | bytes 5019648 | tf_op jit(solution)/shard_map/broadcast_in_dim | solution.py:31
  122.9 0.0 copy-start.1
  122.9 18.3 %fusion.9 = (f32[128]{0:T(128)S(1)}, f32[128,38912]{1,0:T(8,128)}) fusion(bf16[128,256]{1,0:T(8,128)(2,1)S(1)} %all-reduce.2, bf16[256,38912]{1,0:T(8,128)(2,1)} %all-gather.2.cloned.1.call-done, s32[128]{0:T(128)S(1)} %broadcast_subtract_fusion, pred[16,8,304,128]{3,2,1,0:T(8,128)(4,1)S(1)} %bitcast.28), kind=kOutput, calls=%fused_computation.22 | convolution fusion | flops 2570059776 | bytes 44893184 | tf_op jit(solution)/shard_map/dot_general | solution.py:28
  141.2 0.0 copy-done.1
  141.2 4.9 %pmax.7 = f32[128]{0:T(128)S(1)} all-reduce(f32[128]{0:T(128)S(1)} %get-tuple-element.2), channel_id=1, replica_groups=mesh['dp'=16,'vocab'=2] {'vocab'}, use_global_device_ids=true, to_apply=%region_2.3 | all-reduce | flops 128 | bytes 1024 | tf_op jit(solution)/shard_map/pmax | solution.py:37
  146.1 12.7 %fusion.1 = f32[128]{0:T(128)S(1)} fusion(f32[128,38912]{1,0:T(8,128)} %get-tuple-element.3, f32[128]{0:T(128)S(1)} %pmax.7, s32[128]{0:T(128)S(1)} %broadcast_subtract_fusion, pred[16,8,304,128]{3,2,1,0:T(8,128)(4,1)} %bitcast.29), kind=kLoop, calls=%fused_computation.6 | loop fusion | flops 24903552 | bytes 24905216 | tf_op jit(solution)/shard_map/reduce_sum | solution.py:39
  158.9 4.9 %psum.22 = f32[128]{0:T(128)S(1)} all-reduce(f32[128]{0:T(128)S(1)} %fusion.1), channel_id=1, replica_groups=mesh['dp'=16,'vocab'=2] {'vocab'}, use_global_device_ids=true, to_apply=%region_4.5 | all-reduce | flops 128 | bytes 1024 | tf_op jit(solution)/shard_map/psum | solution.py:39
  163.8 0.0 copy-start.2
  163.8 0.0 copy-start.3
  163.8 17.9 %fusion.2 = f32[128,256]{1,0:T(8,128)S(1)} fusion(bf16[256,38912]{1,0:T(8,128)(2,1)} %all-gather.2.cloned.1.call-done, f32[128,38912]{1,0:T(8,128)} %get-tuple-element.3, f32[128]{0:T(128)S(1)} %psum.22, f32[128]{0:T(128)S(1)} %pmax.7, s32[128]{0:T(128)S(1)} %broadcast_subtract_fusion, f32[128]{0:T(128)S(1)} %multiply_multiply_fusion, ...), kind=kOutput, calls=%fused_computation.7 | convolution fusion | flops 2594963456 | bytes 44959744 | tf_op jit(solution)/shard_map/dot_general | solution.py:44
  181.8 9.7 %all-reduce.3 = bf16[128,256]{1,0:T(8,128)(2,1)S(1)} all-reduce(f32[128,256]{1,0:T(8,128)S(1)} %fusion.2), channel_id=1, replica_groups=mesh['dp'=16,'vocab'=2] {'vocab'}, use_global_device_ids=true, to_apply=%region_5.6 | all-reduce | flops 32768 | bytes 196608 | tf_op jit(solution)/shard_map/psum | solution.py:47
  191.5 0.0 copy-done.2
  191.5 2.1 convolution_convert_fusion
  193.6 0.0 reduce-scatter.2.cloned.1.call-update
  193.6 0.0 copy-done.3
  193.6 0.1 broadcast_in_dim.36
  193.7 0.8 gather_fusion
  194.6 0.1 bitcast_select_fusion
  194.7 11.4 %all_to_all.5 = bf16[16,8,256]{2,1,0:T(8,128)(2,1)S(1)} all-to-all(bf16[16,8,256]{2,1,0:T(8,128)(2,1)S(1)} %bitcast_select_fusion), channel_id=1, replica_groups=mesh['dp'=16,'vocab'=2] {'dp'}, dimensions={0} | all-to-all | bytes 131072 | tf_op jit(solution)/shard_map/all_to_all | solution.py:57
  206.1 1.4 convolution_convert_fusion.1
  207.5 47.4 %reduce-scatter.2.cloned.1.call-done = bf16[16,4096]{1,0:T(8,128)(2,1)} async-done(((bf16[256,4096]{1,0:T(8,128)(2,1)}), bf16[16,4096]{1,0:T(8,128)(2,1)}) %reduce-scatter.2.cloned.1.call-update) | async-done | bytes 131088 | tf_op jit(solution)/shard_map/reduce_scatter | solution.py:48
  254.9 1.6 convert_element_type.35
  (6 shorter events, 0.1 us)
Async XLA Ops:
  7.2 2.2 copy-start
  7.2 109.1 %all-gather.2.cloned.1.call-start = ((), (), s32[]{:S(2)}) async-start(), calls=%async_computation.2 | async-start | bytes 21168128 | tf_op jit(solution)/shard_map/all_gather | solution.py:18
  7.9 247.0 %reduce-scatter.2.cloned.1.call-start = ((), (), s32[]{:S(2)}) async-start(), calls=%async_computation.3 | async-start | bytes 2228224 | tf_op jit(solution)/shard_map/reduce_scatter | solution.py:48
  122.9 18.3 %copy-start.1 = (pred[128,304,128]{2,1,0:T(8,128)(4,1)}, pred[128,304,128]{2,1,0:T(8,128)(4,1)S(1)}, u32[]{:S(2)}) copy-start(pred[128,304,128]{2,1,0:T(8,128)(4,1)S(1)} %broadcast_in_dim.39) | copy-start | bytes 14942212
  163.8 27.7 %copy-start.2 = (bf16[128,4096]{1,0:T(8,128)(2,1)S(1)}, bf16[128,4096]{1,0:T(8,128)(2,1)}, u32[]{:S(2)}) copy-start(bf16[128,4096]{1,0:T(8,128)(2,1)} %param.8) | copy-start | bytes 3145732
  163.8 29.8 %copy-start.3 = (s32[128]{0:T(128)S(1)}, s32[128]{0:T(128)}, u32[]{:S(2)}) copy-start(s32[128]{0:T(128)} %param.15) | copy-start | bytes 1540
Sparse Core Ops, SparseCore 0:
  9.6 106.5 all-gather.1
  193.7 61.1 reduce-scatter.1
where the time goes:
time: 264 us; the launch traced here: 263 us
  waiting for transfers between devices  140 us (53%)
  blocking collectives  42.4 us (16%)
  matrix products  41.8 us (16%)
  other arithmetic  15.9 us (6%)
  between operations  14.2 us (5%)
  local copies, waits for them, and re-layouts  8.79 us (3%)
    all_gather x1, waiting for transfers between devices, body(): factor = lax.all_gather(vocab_factor, 'dp', axis=0, tiled=True)  92 us
    reduce_scatter x1, waiting for transfers between devices, body(): lax.psum_scatter(lax.dot_general(rank_grad, hidden, (((0,), (0,)), ((), (...  47.4 us
    dot_general x1, matrix products, body(): logits = jnp.dot(latent, factor, preferred_element_type=jnp.float32)  18.3 us
    dot_general x1, matrix products, body(): lax.dot_general(score_grad, factor, (((1,), (1,)), ((), ())), preferred_e...  17.9 us
    reduce_sum x1, other arithmetic, body(): total = lax.psum(jnp.sum(powers, axis=1), 'vocab')  12.7 us
    psum x1, blocking collectives, body(): latent = lax.psum(partial_latent, 'vocab').astype(jnp.bfloat16)  11.4 us
    all_to_all x1, blocking collectives, body(): lax.all_to_all(picked, 'dp', split_axis=0, concat_axis=0, tiled=True)  11.4 us
    psum x1, blocking collectives, body(): rank_grad = lax.psum(rank_partial, 'vocab').astype(jnp.bfloat16)  9.72 us
  transfers between devices with their start and end apart: 2, of which 2 were waited for; matrix products, arithmetic and copies ran while one was open for 3% of the time, Pallas kernels for 0%

commit v1 on v0

--- a/solution.py
+++ b/solution.py
@@ -8,6 +8,25 @@
 
 
 def body(hidden, rank_factor, vocab_factor, lengths, targets, cotangent, grammar, assign):
+
+    def divide_digits(t0):
+        amount_of = lax.psum(1, axis_name="dp")
+        windows = []
+        kk = 1
+        while kk < amount_of:
+            windows.append((kk - 1, kk))
+            kk = kk + 1
+        arr_next = windows + [(amount_of - 1, 0)]
+        plain = t0
+        series = [plain]
+        idx = 0
+        while idx < amount_of - 1:
+            plain = lax.ppermute(plain, axis_name="dp", perm=arr_next)
+            series += [plain]
+            idx += 1
+        finding = jnp.concatenate([*reversed(series)], axis=0)
+        return jnp.roll(finding, (lax.axis_index("dp") + 1) * plain.shape[0], axis=0)
+
     row_count = hidden.shape[0]
     rank = rank_factor.shape[0]
     groups = lax.axis_size("dp")
@@ -15,7 +34,7 @@
     width = vocab_factor.shape[1]
     tiles = width // 128
     first = lax.axis_index("vocab") * width
-    factor = lax.all_gather(vocab_factor, "dp", axis=0, tiled=True)
+    factor = divide_digits(vocab_factor)
     row_words = jnp.repeat(grammar, row_count // grammar.shape[0], axis=0)
     weight = cotangent.astype(jnp.float32) * lengths.astype(jnp.float32) / PREFIX_MAX
     partial_latent = lax.dot_general(

time: 264 us -> 503 us (1.91)
  waiting for transfers between devices: 140 us -> 316 us
  local copies, waits for them, and re-layouts: 8.79 us -> 73.3 us
    ppermute x0 -> x15, waiting for transfers between devices: none -> 270 us  [divide_digits(): plain = lax.ppermute(plain, axis_name='dp', perm=arr_next)]
    all_gather x1 -> x0, waiting for transfers between devices: 92 us -> none  [body(): factor = lax.all_gather(vocab_factor, 'dp', axis=0, tiled=True)]
    unnamed x9 -> x94, local copies, waits for them, and re-layouts: 0.79 us -> 63.4 us
  transfers between devices with their start and end apart: 2 -> 16, of which waited for: 2 -> 16; matrix products, arithmetic and copies ran while one was open for 3% -> 2% of each run, Pallas kernels for 0% -> 0%
where the time goes in v1:
time: 503 us
  waiting for transfers between devices  316 us (63%)
  local copies, waits for them, and re-layouts  73.3 us (15%)
  matrix products  41.6 us (8%)
  blocking collectives  40.5 us (8%)
  other arithmetic  16.5 us (3%)
  between operations  14.3 us (3%)
    ppermute x15, waiting for transfers between devices, divide_digits(): plain = lax.ppermute(plain, axis_name='dp', perm=arr_next)  270 us
    unnamed x94, local copies, waits for them, and re-layouts  63.4 us
    reduce_scatter x1, waiting for transfers between devices, body(): lax.psum_scatter(lax.dot_general(rank_grad, hidden, (((0,), (0,)), ((), (...  45.6 us
    dot_general x1, matrix products, body(): lax.dot_general(score_grad, factor, (((1,), (1,)), ((), ())), preferred_e...  18 us
    dot_general x1, matrix products, body(): logits = jnp.dot(latent, factor, preferred_element_type=jnp.float32)  18 us
    reduce_sum x1, other arithmetic, body(): total = lax.psum(jnp.sum(powers, axis=1), 'vocab')  12.7 us
    psum x1, blocking collectives, body(): latent = lax.psum(partial_latent, 'vocab').astype(jnp.bfloat16)  10.7 us
    psum x1, blocking collectives, body(): rank_grad = lax.psum(rank_partial, 'vocab').astype(jnp.bfloat16)  10.2 us
  transfers between devices with their start and end apart: 16, of which 16 were waited for; matrix products, arithmetic and copies ran while one was open for 2% of the time, Pallas kernels for 0%

profile of v1, /device:TPU:0, one launch (start us, length us, event | category | flops | bytes accessed | tf_op | source)
XLA Modules:
  0.0 502.6 jit_solution(8616262611723640237)
XLA Ops:
  7.7 19.8 %collective-permute-done = bf16[16,38912]{1,0:T(8,128)(2,1)S(1)} collective-permute-done((bf16[16,38912]{1,0:T(8,128)(2,1)}, bf16[16,38912]{1,0:T(8,128)(2,1)S(1)}, u32[]{:S(2)}, u32[]{:S(2)}) %collective-permute-start) | collective-permute-done | bytes 1245216 | tf_op jit(solution)/shard_map/ppermute | solution.py:24
  28.6 19.0 %collective-permute-done.1 = bf16[16,38912]{1,0:T(8,128)(2,1)S(1)} collective-permute-done((bf16[16,38912]{1,0:T(8,128)(2,1)S(1)}, bf16[16,38912]{1,0:T(8,128)(2,1)S(1)}, u32[]{:S(2)}, u32[]{:S(2)}) %collective-permute-start.1) | collective-permute-done | bytes 1245216 | tf_op jit(solution)/shard_map/ppermute | solution.py:24
  48.6 19.0 %collective-permute-done.2 = bf16[16,38912]{1,0:T(8,128)(2,1)S(1)} collective-permute-done((bf16[16,38912]{1,0:T(8,128)(2,1)S(1)}, bf16[16,38912]{1,0:T(8,128)(2,1)S(1)}, u32[]{:S(2)}, u32[]{:S(2)}) %collective-permute-start.2) | collective-permute-done | bytes 1245216 | tf_op jit(solution)/shard_map/ppermute | solution.py:24
  68.7 19.0 %collective-permute-done.3 = bf16[16,38912]{1,0:T(8,128)(2,1)S(1)} collective-permute-done((bf16[16,38912]{1,0:T(8,128)(2,1)S(1)}, bf16[16,38912]{1,0:T(8,128)(2,1)S(1)}, u32[]{:S(2)}, u32[]{:S(2)}) %collective-permute-start.3) | collective-permute-done | bytes 1245216 | tf_op jit(solution)/shard_map/ppermute | solution.py:24
  88.8 19.0 %collective-permute-done.4 = bf16[16,38912]{1,0:T(8,128)(2,1)S(1)} collective-permute-done((bf16[16,38912]{1,0:T(8,128)(2,1)S(1)}, bf16[16,38912]{1,0:T(8,128)(2,1)S(1)}, u32[]{:S(2)}, u32[]{:S(2)}) %collective-permute-start.4) | collective-permute-done | bytes 1245216 | tf_op jit(solution)/shard_map/ppermute | solution.py:24
  108.9 19.0 %collective-permute-done.5 = bf16[16,38912]{1,0:T(8,128)(2,1)S(1)} collective-permute-done((bf16[16,38912]{1,0:T(8,128)(2,1)S(1)}, bf16[16,38912]{1,0:T(8,128)(2,1)S(1)}, u32[]{:S(2)}, u32[]{:S(2)}) %collective-permute-start.5) | collective-permute-done | bytes 1245216 | tf_op jit(solution)/shard_map/ppermute | solution.py:24
  129.0 19.0 %collective-permute-done.6 = bf16[16,38912]{1,0:T(8,128)(2,1)S(1)} collective-permute-done((bf16[16,38912]{1,0:T(8,128)(2,1)S(1)}, bf16[16,38912]{1,0:T(8,128)(2,1)S(1)}, u32[]{:S(2)}, u32[]{:S(2)}) %collective-permute-start.6) | collective-permute-done | bytes 1245216 | tf_op jit(solution)/shard_map/ppermute | solution.py:24
  149.1 19.0 %collective-permute-done.7 = bf16[16,38912]{1,0:T(8,128)(2,1)S(1)} collective-permute-done((bf16[16,38912]{1,0:T(8,128)(2,1)S(1)}, bf16[16,38912]{1,0:T(8,128)(2,1)S(1)}, u32[]{:S(2)}, u32[]{:S(2)}) %collective-permute-start.7) | collective-permute-done | bytes 1245216 | tf_op jit(solution)/shard_map/ppermute | solution.py:24
  169.1 19.0 %collective-permute-done.8 = bf16[16,38912]{1,0:T(8,128)(2,1)S(1)} collective-permute-done((bf16[16,38912]{1,0:T(8,128)(2,1)S(1)}, bf16[16,38912]{1,0:T(8,128)(2,1)S(1)}, u32[]{:S(2)}, u32[]{:S(2)}) %collective-permute-start.8) | collective-permute-done | bytes 1245216 | tf_op jit(solution)/shard_map/ppermute | solution.py:24
  189.2 19.0 %collective-permute-done.9 = bf16[16,38912]{1,0:T(8,128)(2,1)S(1)} collective-permute-done((bf16[16,38912]{1,0:T(8,128)(2,1)S(1)}, bf16[16,38912]{1,0:T(8,128)(2,1)S(1)}, u32[]{:S(2)}, u32[]{:S(2)}) %collective-permute-start.9) | collective-permute-done | bytes 1245216 | tf_op jit(solution)/shard_map/ppermute | solution.py:24
  209.3 19.0 %collective-permute-done.10 = bf16[16,38912]{1,0:T(8,128)(2,1)S(1)} collective-permute-done((bf16[16,38912]{1,0:T(8,128)(2,1)S(1)}, bf16[16,38912]{1,0:T(8,128)(2,1)S(1)}, u32[]{:S(2)}, u32[]{:S(2)}) %collective-permute-start.10) | collective-permute-done | bytes 1245216 | tf_op jit(solution)/shard_map/ppermute | solution.py:24
  229.4 19.0 %collective-permute-done.11 = bf16[16,38912]{1,0:T(8,128)(2,1)S(1)} collective-permute-done((bf16[16,38912]{1,0:T(8,128)(2,1)S(1)}, bf16[16,38912]{1,0:T(8,128)(2,1)S(1)}, u32[]{:S(2)}, u32[]{:S(2)}) %collective-permute-start.11) | collective-permute-done | bytes 1245216 | tf_op jit(solution)/shard_map/ppermute | solution.py:24
  249.5 19.0 %collective-permute-done.12 = bf16[16,38912]{1,0:T(8,128)(2,1)S(1)} collective-permute-done((bf16[16,38912]{1,0:T(8,128)(2,1)S(1)}, bf16[16,38912]{1,0:T(8,128)(2,1)S(1)}, u32[]{:S(2)}, u32[]{:S(2)}) %collective-permute-start.12) | collective-permute-done | bytes 1245216 | tf_op jit(solution)/shard_map/ppermute | solution.py:24
  269.5 19.1 %collective-permute-done.13 = bf16[16,38912]{1,0:T(8,128)(2,1)} collective-permute-done((bf16[16,38912]{1,0:T(8,128)(2,1)S(1)}, bf16[16,38912]{1,0:T(8,128)(2,1)}, u32[]{:S(2)}, u32[]{:S(2)}) %collective-permute-start.13) | collective-permute-done | bytes 1245216 | tf_op jit(solution)/shard_map/ppermute | solution.py:24
  290.0 2.2 fusion.14
  292.2 10.7 %all-reduce.2 = bf16[128,256]{1,0:T(8,128)(2,1)} all-reduce(f32[128,256]{1,0:T(8,128)S(1)} %fusion.14), channel_id=1, replica_groups=mesh['dp'=16,'vocab'=2] {'vocab'}, use_global_device_ids=true, to_apply=%region_0.1 | all-reduce | flops 32768 | bytes 196608 | tf_op jit(solution)/shard_map/psum | solution.py:43
  304.9 3.1 collective-permute-done.14
  308.0 2.4 constant_dynamic-update-slice_fusion.31
  310.4 2.4 constant_dynamic-update-slice_fusion.30
  312.8 2.5 constant_dynamic-update-slice_fusion.29
  315.3 2.5 constant_dynamic-update-slice_fusion.28
  317.9 2.6 constant_dynamic-update-slice_fusion.27
  320.4 2.5 constant_dynamic-update-slice_fusion.26
  322.9 2.6 constant_dynamic-update-slice_fusion.25
  325.5 2.5 constant_dynamic-update-slice_fusion.24
  330.3 1.2 constant_dynamic-update-slice_fusion.21
  332.6 1.2 constant_dynamic-update-slice_fusion.19
  334.8 1.2 constant_dynamic-update-slice_fusion.17
  337.1 2.4 constant_dynamic-update-slice_fusion.15
  339.6 2.5 constant_dynamic-update-slice_fusion.14
  342.0 1.2 constant_dynamic-update-slice_fusion.13
  343.2 1.2 constant_dynamic-update-slice_fusion.12
  344.4 1.2 constant_dynamic-update-slice_fusion.11
  347.9 1.2 constant_dynamic-update-slice_fusion.8
  351.3 1.1 constant_dynamic-update-slice_fusion.5
  354.7 1.2 constant_dynamic-update-slice_fusion.2
  358.1 7.4 %broadcast_in_dim.39 = pred[128,304,128]{2,1,0:T(8,128)(4,1)} broadcast(pred[128,304]{1,0:T(8,128)(4,1)S(1)} %copy.11), dimensions={0,1} | broadcast | bytes 5019648 | tf_op jit(solution)/shard_map/broadcast_in_dim | solution.py:50
  365.5 18.0 %fusion.13 = (f32[128]{0:T(128)S(1)}, f32[128,38912]{1,0:T(8,128)}) fusion(bf16[128,256]{1,0:T(8,128)(2,1)S(1)} %copy-done.29, bf16[512,38912]{1,0:T(8,128)(2,1)} %constant_dynamic-update-slice_fusion, s32[]{:T(128)S(6)} %select_n.32, s32[128]{0:T(128)S(1)} %broadcast_subtract_fusion, pred[16,8,304,128]{3,2,1,0:T(8,128)(4,1)} %bitcast.26), kind=kOutput, calls=%fused_computation.58 | convolution fusion | flops 2570059776 | bytes 44893188 | tf_op jit(solution)/shard_map/dot_general | solution.py:47
  383.4 5.1 %pmax.7 = f32[128]{0:T(128)S(1)} all-reduce(f32[128]{0:T(128)S(1)} %get-tuple-element.2), channel_id=1, replica_groups=mesh['dp'=16,'vocab'=2] {'vocab'}, use_global_device_ids=true, to_apply=%region_2.3 | all-reduce | flops 128 | bytes 1024 | tf_op jit(solution)/shard_map/pmax | solution.py:56
  388.5 12.7 %fusion.4 = f32[128]{0:T(128)S(1)} fusion(f32[128,38912]{1,0:T(8,128)} %get-tuple-element.3, f32[128]{0:T(128)S(1)} %pmax.7, s32[128]{0:T(128)S(1)} %broadcast_subtract_fusion, pred[16,8,304,128]{3,2,1,0:T(8,128)(4,1)} %bitcast.27), kind=kLoop, calls=%fused_computation.9 | loop fusion | flops 24903552 | bytes 24905216 | tf_op jit(solution)/shard_map/reduce_sum | solution.py:58
  401.3 4.9 psum.22
  406.2 18.0 %fusion.1 = f32[128,256]{1,0:T(8,128)S(1)} fusion(bf16[512,38912]{1,0:T(8,128)(2,1)} %constant_dynamic-update-slice_fusion, s32[]{:T(128)S(6)} %select_n.32, f32[128,38912]{1,0:T(8,128)} %get-tuple-element.3, f32[128]{0:T(128)S(1)} %psum.22, f32[128]{0:T(128)S(1)} %pmax.7, s32[128]{0:T(128)S(1)} %broadcast_subtract_fusion, ...), kind=kOutput, calls=%fused_computation.6 | convolution fusion | flops 2594963456 | bytes 44959748 | tf_op jit(solution)/shard_map/dot_general | solution.py:63
  424.2 10.2 %all-reduce.3 = bf16[128,256]{1,0:T(8,128)(2,1)S(1)} all-reduce(f32[128,256]{1,0:T(8,128)S(1)} %fusion.1), channel_id=1, replica_groups=mesh['dp'=16,'vocab'=2] {'vocab'}, use_global_device_ids=true, to_apply=%region_5.6 | all-reduce | flops 32768 | bytes 196608 | tf_op jit(solution)/shard_map/psum | solution.py:66
  434.5 2.1 convolution_convert_fusion
  437.6 9.5 %all_to_all.5 = bf16[16,8,256]{2,1,0:T(8,128)(2,1)S(1)} all-to-all(bf16[16,8,256]{2,1,0:T(8,128)(2,1)S(1)} %bitcast_select_fusion), channel_id=1, replica_groups=mesh['dp'=16,'vocab'=2] {'dp'}, dimensions={0} | all-to-all | bytes 131072 | tf_op jit(solution)/shard_map/all_to_all | solution.py:76
  447.1 1.4 convolution_convert_fusion.1
  448.5 45.6 %reduce-scatter.2.cloned.1.call-done = bf16[16,4096]{1,0:T(8,128)(2,1)} async-done(((bf16[256,4096]{1,0:T(8,128)(2,1)}), bf16[16,4096]{1,0:T(8,128)(2,1)}) %reduce-scatter.2.cloned.1.call-update) | async-done | bytes 131088 | tf_op jit(solution)/shard_map/reduce_scatter | solution.py:67
  494.2 1.6 convert_element_type.35
  (109 shorter events, 33.2 us)
Async XLA Ops:
  7.2 282.8 %copy-start = (bf16[256,4096]{1,0:T(8,128)(2,1)S(1)}, bf16[256,4096]{1,0:T(8,128)(2,1)}, u32[]{:S(2)}) copy-start(bf16[256,4096]{1,0:T(8,128)(2,1)} %param.9) | copy-start | bytes 6291460
  7.2 487.0 %reduce-scatter.2.cloned.1.call-start = ((), (), s32[]{:S(2)}) async-start(), calls=%async_computation.2 | async-start | bytes 2228224 | tf_op jit(solution)/shard_map/reduce_scatter | solution.py:67
  7.2 20.3 %collective-permute-start = (bf16[16,38912]{1,0:T(8,128)(2,1)}, bf16[16,38912]{1,0:T(8,128)(2,1)S(1)}, u32[]{:S(2)}, u32[]{:S(2)}) collective-permute-start(bf16[16,38912]{1,0:T(8,128)(2,1)} %param.10), channel_id=1, source_target_pairs={{0,2},{2,4},{4,6},{6,8},{8,10},{10,12},{12,14},{14,16},{16,18},{18... | collective-permute-start | bytes 3735560 | tf_op jit(solution)/shard_map/ppermute | solution.py:24
  27.5 1.1 copy-start.2
  28.6 19.0 %collective-permute-start.1 = (bf16[16,38912]{1,0:T(8,128)(2,1)S(1)}, bf16[16,38912]{1,0:T(8,128)(2,1)S(1)}, u32[]{:S(2)}, u32[]{:S(2)}) collective-permute-start(bf16[16,38912]{1,0:T(8,128)(2,1)S(1)} %collective-permute-done), channel_id=1, source_target_pairs={{0,2},{2,4},{4,6},{6,8},{8,10},{10,12},{12,14},{14,16},{16,18},{18... | collective-permute-start | bytes 3735560 | tf_op jit(solution)/shard_map/ppermute | solution.py:24
  47.6 1.0 copy-start.4
  48.6 19.0 %collective-permute-start.2 = (bf16[16,38912]{1,0:T(8,128)(2,1)S(1)}, bf16[16,38912]{1,0:T(8,128)(2,1)S(1)}, u32[]{:S(2)}, u32[]{:S(2)}) collective-permute-start(bf16[16,38912]{1,0:T(8,128)(2,1)S(1)} %collective-permute-done.1), channel_id=1, source_target_pairs={{0,2},{2,4},{4,6},{6,8},{8,10},{10,12},{12,14},{14,16},{16,18},{18... | collective-permute-start | bytes 3735560 | tf_op jit(solution)/shard_map/ppermute | solution.py:24
  67.7 1.0 copy-start.6
  68.7 19.0 %collective-permute-start.3 = (bf16[16,38912]{1,0:T(8,128)(2,1)S(1)}, bf16[16,38912]{1,0:T(8,128)(2,1)S(1)}, u32[]{:S(2)}, u32[]{:S(2)}) collective-permute-start(bf16[16,38912]{1,0:T(8,128)(2,1)S(1)} %collective-permute-done.2), channel_id=1, source_target_pairs={{0,2},{2,4},{4,6},{6,8},{8,10},{10,12},{12,14},{14,16},{16,18},{18... | collective-permute-start | bytes 3735560 | tf_op jit(solution)/shard_map/ppermute | solution.py:24
  87.7 1.0 copy-start.8
  88.8 19.0 %collective-permute-start.4 = (bf16[16,38912]{1,0:T(8,128)(2,1)S(1)}, bf16[16,38912]{1,0:T(8,128)(2,1)S(1)}, u32[]{:S(2)}, u32[]{:S(2)}) collective-permute-start(bf16[16,38912]{1,0:T(8,128)(2,1)S(1)} %collective-permute-done.3), channel_id=1, source_target_pairs={{0,2},{2,4},{4,6},{6,8},{8,10},{10,12},{12,14},{14,16},{16,18},{18... | collective-permute-start | bytes 3735560 | tf_op jit(solution)/shard_map/ppermute | solution.py:24
  107.8 1.1 copy-start.10
  108.9 19.0 %collective-permute-start.5 = (bf16[16,38912]{1,0:T(8,128)(2,1)S(1)}, bf16[16,38912]{1,0:T(8,128)(2,1)S(1)}, u32[]{:S(2)}, u32[]{:S(2)}) collective-permute-start(bf16[16,38912]{1,0:T(8,128)(2,1)S(1)} %collective-permute-done.4), channel_id=1, source_target_pairs={{0,2},{2,4},{4,6},{6,8},{8,10},{10,12},{12,14},{14,16},{16,18},{18... | collective-permute-start | bytes 3735560 | tf_op jit(solution)/shard_map/ppermute | solution.py:24
  127.9 1.1 copy-start.12
  128.9 19.0 %collective-permute-start.6 = (bf16[16,38912]{1,0:T(8,128)(2,1)S(1)}, bf16[16,38912]{1,0:T(8,128)(2,1)S(1)}, u32[]{:S(2)}, u32[]{:S(2)}) collective-permute-start(bf16[16,38912]{1,0:T(8,128)(2,1)S(1)} %collective-permute-done.5), channel_id=1, source_target_pairs={{0,2},{2,4},{4,6},{6,8},{8,10},{10,12},{12,14},{14,16},{16,18},{18... | collective-permute-start | bytes 3735560 | tf_op jit(solution)/shard_map/ppermute | solution.py:24
  148.0 1.1 copy-start.14
  149.1 19.0 %collective-permute-start.7 = (bf16[16,38912]{1,0:T(8,128)(2,1)S(1)}, bf16[16,38912]{1,0:T(8,128)(2,1)S(1)}, u32[]{:S(2)}, u32[]{:S(2)}) collective-permute-start(bf16[16,38912]{1,0:T(8,128)(2,1)S(1)} %collective-permute-done.6), channel_id=1, source_target_pairs={{0,2},{2,4},{4,6},{6,8},{8,10},{10,12},{12,14},{14,16},{16,18},{18... | collective-permute-start | bytes 3735560 | tf_op jit(solution)/shard_map/ppermute | solution.py:24
  168.1 1.0 copy-start.16
  169.1 19.0 %collective-permute-start.8 = (bf16[16,38912]{1,0:T(8,128)(2,1)S(1)}, bf16[16,38912]{1,0:T(8,128)(2,1)S(1)}, u32[]{:S(2)}, u32[]{:S(2)}) collective-permute-start(bf16[16,38912]{1,0:T(8,128)(2,1)S(1)} %collective-permute-done.7), channel_id=1, source_target_pairs={{0,2},{2,4},{4,6},{6,8},{8,10},{10,12},{12,14},{14,16},{16,18},{18... | collective-permute-start | bytes 3735560 | tf_op jit(solution)/shard_map/ppermute | solution.py:24
  188.2 1.1 copy-start.18
  189.2 19.0 %collective-permute-start.9 = (bf16[16,38912]{1,0:T(8,128)(2,1)S(1)}, bf16[16,38912]{1,0:T(8,128)(2,1)S(1)}, u32[]{:S(2)}, u32[]{:S(2)}) collective-permute-start(bf16[16,38912]{1,0:T(8,128)(2,1)S(1)} %collective-permute-done.8), channel_id=1, source_target_pairs={{0,2},{2,4},{4,6},{6,8},{8,10},{10,12},{12,14},{14,16},{16,18},{18... | collective-permute-start | bytes 3735560 | tf_op jit(solution)/shard_map/ppermute | solution.py:24
  208.3 1.1 copy-start.20
  209.3 19.0 %collective-permute-start.10 = (bf16[16,38912]{1,0:T(8,128)(2,1)S(1)}, bf16[16,38912]{1,0:T(8,128)(2,1)S(1)}, u32[]{:S(2)}, u32[]{:S(2)}) collective-permute-start(bf16[16,38912]{1,0:T(8,128)(2,1)S(1)} %collective-permute-done.9), channel_id=1, source_target_pairs={{0,2},{2,4},{4,6},{6,8},{8,10},{10,12},{12,14},{14,16},{16,18},{18... | collective-permute-start | bytes 3735560 | tf_op jit(solution)/shard_map/ppermute | solution.py:24
  228.4 1.0 copy-start.22
  229.4 19.0 %collective-permute-start.11 = (bf16[16,38912]{1,0:T(8,128)(2,1)S(1)}, bf16[16,38912]{1,0:T(8,128)(2,1)S(1)}, u32[]{:S(2)}, u32[]{:S(2)}) collective-permute-start(bf16[16,38912]{1,0:T(8,128)(2,1)S(1)} %collective-permute-done.10), channel_id=1, source_target_pairs={{0,2},{2,4},{4,6},{6,8},{8,10},{10,12},{12,14},{14,16},{16,18},{18... | collective-permute-start | bytes 3735560 | tf_op jit(solution)/shard_map/ppermute | solution.py:24
  248.4 1.0 copy-start.24
  249.5 19.0 %collective-permute-start.12 = (bf16[16,38912]{1,0:T(8,128)(2,1)S(1)}, bf16[16,38912]{1,0:T(8,128)(2,1)S(1)}, u32[]{:S(2)}, u32[]{:S(2)}) collective-permute-start(bf16[16,38912]{1,0:T(8,128)(2,1)S(1)} %collective-permute-done.11), channel_id=1, source_target_pairs={{0,2},{2,4},{4,6},{6,8},{8,10},{10,12},{12,14},{14,16},{16,18},{18... | collective-permute-start | bytes 3735560 | tf_op jit(solution)/shard_map/ppermute | solution.py:24
  268.5 1.0 copy-start.26
  269.5 19.1 %collective-permute-start.13 = (bf16[16,38912]{1,0:T(8,128)(2,1)S(1)}, bf16[16,38912]{1,0:T(8,128)(2,1)}, u32[]{:S(2)}, u32[]{:S(2)}) collective-permute-start(bf16[16,38912]{1,0:T(8,128)(2,1)S(1)} %collective-permute-done.12), channel_id=1, source_target_pairs={{0,2},{2,4},{4,6},{6,8},{8,10},{10,12},{12,14},{14,16},{16,18},{18... | collective-permute-start | bytes 3735560 | tf_op jit(solution)/shard_map/ppermute | solution.py:24
  288.7 19.3 %collective-permute-start.14 = (bf16[16,38912]{1,0:T(8,128)(2,1)}, bf16[16,38912]{1,0:T(8,128)(2,1)}, u32[]{:S(2)}, u32[]{:S(2)}) collective-permute-start(bf16[16,38912]{1,0:T(8,128)(2,1)} %collective-permute-done.13), channel_id=1, source_target_pairs={{0,2},{2,4},{4,6},{6,8},{8,10},{10,12},{12,14},{14,16},{16,18},{18... | collective-permute-start | bytes 3735560 | tf_op jit(solution)/shard_map/ppermute | solution.py:24
  290.0 46.0 %copy-start.1 = (bf16[16,38912]{1,0:T(8,128)(2,1)S(1)}, bf16[16,38912]{1,0:T(8,128)(2,1)}, u32[]{:S(2)}) copy-start(bf16[16,38912]{1,0:T(8,128)(2,1)} %param.10) | copy-start | bytes 3735556
  302.9 25.1 %copy-start.15 = (bf16[16,38912]{1,0:T(8,128)(2,1)S(1)}, bf16[16,38912]{1,0:T(8,128)(2,1)}, u32[]{:S(2)}) copy-start(bf16[16,38912]{1,0:T(8,128)(2,1)} %copy-done.14) | copy-start | bytes 3735556
  302.9 26.2 %copy-start.13 = (bf16[16,38912]{1,0:T(8,128)(2,1)S(1)}, bf16[16,38912]{1,0:T(8,128)(2,1)}, u32[]{:S(2)}) copy-start(bf16[16,38912]{1,0:T(8,128)(2,1)} %copy-done.12) | copy-start | bytes 3735556
  302.9 27.4 %copy-start.11 = (bf16[16,38912]{1,0:T(8,128)(2,1)S(1)}, bf16[16,38912]{1,0:T(8,128)(2,1)}, u32[]{:S(2)}) copy-start(bf16[16,38912]{1,0:T(8,128)(2,1)} %copy-done.10) | copy-start | bytes 3735556
  302.9 28.5 %copy-start.9 = (bf16[16,38912]{1,0:T(8,128)(2,1)S(1)}, bf16[16,38912]{1,0:T(8,128)(2,1)}, u32[]{:S(2)}) copy-start(bf16[16,38912]{1,0:T(8,128)(2,1)} %copy-done.8) | copy-start | bytes 3735556
  302.9 29.6 %copy-start.7 = (bf16[16,38912]{1,0:T(8,128)(2,1)S(1)}, bf16[16,38912]{1,0:T(8,128)(2,1)}, u32[]{:S(2)}) copy-start(bf16[16,38912]{1,0:T(8,128)(2,1)} %copy-done.6) | copy-start | bytes 3735556
  302.9 30.8 %copy-start.5 = (bf16[16,38912]{1,0:T(8,128)(2,1)S(1)}, bf16[16,38912]{1,0:T(8,128)(2,1)}, u32[]{:S(2)}) copy-start(bf16[16,38912]{1,0:T(8,128)(2,1)} %copy-done.4) | copy-start | bytes 3735556
  303.0 31.9 %copy-start.3 = (bf16[16,38912]{1,0:T(8,128)(2,1)S(1)}, bf16[16,38912]{1,0:T(8,128)(2,1)}, u32[]{:S(2)}) copy-start(bf16[16,38912]{1,0:T(8,128)(2,1)} %copy-done.2) | copy-start | bytes 3735556
  312.8 29.2 %copy-start.27 = (bf16[16,38912]{1,0:T(8,128)(2,1)S(1)}, bf16[16,38912]{1,0:T(8,128)(2,1)}, u32[]{:S(2)}) copy-start(bf16[16,38912]{1,0:T(8,128)(2,1)} %copy-done.26) | copy-start | bytes 3735556
  315.3 27.9 %copy-start.25 = (bf16[16,38912]{1,0:T(8,128)(2,1)S(1)}, bf16[16,38912]{1,0:T(8,128)(2,1)}, u32[]{:S(2)}) copy-start(bf16[16,38912]{1,0:T(8,128)(2,1)} %copy-done.24) | copy-start | bytes 3735556
  317.8 26.5 %copy-start.23 = (bf16[16,38912]{1,0:T(8,128)(2,1)S(1)}, bf16[16,38912]{1,0:T(8,128)(2,1)}, u32[]{:S(2)}) copy-start(bf16[16,38912]{1,0:T(8,128)(2,1)} %copy-done.22) | copy-start | bytes 3735556
  320.4 25.2 %copy-start.21 = (bf16[16,38912]{1,0:T(8,128)(2,1)S(1)}, bf16[16,38912]{1,0:T(8,128)(2,1)}, u32[]{:S(2)}) copy-start(bf16[16,38912]{1,0:T(8,128)(2,1)} %copy-done.20) | copy-start | bytes 3735556
  322.9 23.8 %copy-start.19 = (bf16[16,38912]{1,0:T(8,128)(2,1)S(1)}, bf16[16,38912]{1,0:T(8,128)(2,1)}, u32[]{:S(2)}) copy-start(bf16[16,38912]{1,0:T(8,128)(2,1)} %copy-done.18) | copy-start | bytes 3735556
  325.5 22.3 %copy-start.17 = (bf16[16,38912]{1,0:T(8,128)(2,1)S(1)}, bf16[16,38912]{1,0:T(8,128)(2,1)}, u32[]{:S(2)}) copy-start(bf16[16,38912]{1,0:T(8,128)(2,1)} %copy-done.16) | copy-start | bytes 3735556
  342.0 23.4 %copy-start.29 = (bf16[128,256]{1,0:T(8,128)(2,1)S(1)}, bf16[128,256]{1,0:T(8,128)(2,1)}, u32[]{:S(2)}) copy-start(bf16[128,256]{1,0:T(8,128)(2,1)} %all-reduce.2) | copy-start | bytes 196612
  406.2 28.2 %copy-start.28 = (bf16[128,4096]{1,0:T(8,128)(2,1)S(1)}, bf16[128,4096]{1,0:T(8,128)(2,1)}, u32[]{:S(2)}) copy-start(bf16[128,4096]{1,0:T(8,128)(2,1)} %param.8) | copy-start | bytes 3145732
  406.2 30.4 %copy-start.30 = (s32[128]{0:T(128)S(1)}, s32[128]{0:T(128)}, u32[]{:S(2)}) copy-start(s32[128]{0:T(128)} %param.15) | copy-start | bytes 1540
Sparse Core Ops, SparseCore 0:
  436.7 57.4 reduce-scatter.1
